TPU v7x, 128 devices: a whole 4x4x4 slice. The times are simulated.
128 devices in a mesh: dp: 8 (over z, core), expert: 16 (over x, y).
Axes of the slice: x: 4, y: 4, z: 4, core: 2. Of those that a mesh axis runs over, the one named last changes fastest.
Arguments:
- residual_in: bfloat16 [8192, 2048], P(('dp', 'expert')), may hold values from -40 to 40
- attention_gain: float32 [2048], replicated, may hold values from 0.25 to 1.75
- query_weight: bfloat16 [2048, 2048], P(None, 'expert'), may hold values from -0.125 to 0.125
- key_weight: bfloat16 [2048, 2048], P(None, 'expert'), may hold values from -0.125 to 0.125
- value_weight: bfloat16 [2048, 2048], P(None, 'expert'), may hold values from -0.125 to 0.125
- output_weight: bfloat16 [2048, 2048], P('expert'), may hold values from -0.125 to 0.125
- prompt_keys: bfloat16 [24, 2048, 2048], P('dp', None, 'expert'), may hold values from -220 to 220
- prompt_values: bfloat16 [24, 2048, 2048], P('dp', None, 'expert'), may hold values from -12 to 12
- group_index: int32 [8, 32], P('dp'), may hold values from 0 to 2, never falling along the last dimension, each value on 1 to 16 neighbouring positions
- prompt_length: int32 [24], P('dp'), may hold values from 1 to 2048, 24576 in all
- own_length: int32 [256], P('dp'), may hold values from 1 to 32
- expert_gain: float32 [2048], replicated, may hold values from 0.25 to 1.75
- expert_ids: int32 [8192, 8], P(('dp', 'expert')), may hold values from 0 to 63, all different within a row; in each aligned block of 64 rows (0 to 63, 64 to 127, ...) at most 12 rows name the same one
- expert_mix: float32 [8192, 8], P(('dp', 'expert')), may hold values from 0.02 to 0.3
- gate_weight: bfloat16 [128, 2048, 512], P(('dp', 'expert')), may hold values from -0.125 to 0.125
- up_weight: bfloat16 [128, 2048, 512], P(('dp', 'expert')), may hold values from -0.125 to 0.125
- down_weight: bfloat16 [128, 512, 2048], P(('dp', 'expert')), may hold values from -0.1875 to 0.1875
Outputs:
- attention_update: bfloat16 [8192, 2048], P(('dp', 'expert'))
- expert_update: bfloat16 [8192, 2048], P(('dp', 'expert'))
Inputs may be any that keep to these rules, and one draw needn't show every extreme that they name: `group_index`: each row holds the 32 requests of one index of dp; a group's requests are consecutive, every group has 1 to 16 requests and some group exactly 16. `prompt_length`: some prompt is exactly 2048 long. `expert_ids`: a token's 8 experts differ; among the 64 rows of one device no expert is named more than 12 times, a bound that some block reaches.
All inputs are finite; a program needn't handle non-finite values. No bound on the sum of `prompt_length` on one device may be relied on, other than what follows from the above.
Results may differ from a plain program's by a relative error of at most 0.025.
The roundings to bfloat16 on the way count: a program that leaves them out, or rounds other values in their place, can miss the bound.
Values may be sent and summed in bfloat16 or wider, within the bound.
No kernel may reach another device: no remote copies, remote signals or barrier semaphores. Data moves between devices by JAX's collectives and lax.ppermute only.
A program may use at most 128 MiB of HBM per device.

v0:
```python
import jax
import jax.numpy as jnp
from jax import lax
from jax.sharding import PartitionSpec as P

HD = 128
FF = 1024
TOP = 8
GSIZE = 16
SB = 32
epsilon = 1e-06


def rms_scale(values, gain):
    widened = values.astype(jnp.float32)
    spread = jnp.mean(widened * widened, axis=-1, keepdims=True)
    return (widened * lax.rsqrt(spread + epsilon) * gain).astype(jnp.bfloat16)


def expert_block(block, gate_weight, up_weight, down_weight):
    shape_kept = block.shape
    flat = block.reshape(-1, shape_kept[-1])
    gated = jnp.dot(flat, gate_weight[0], preferred_element_type=jnp.float32)
    lifted = jnp.dot(flat, up_weight[0], preferred_element_type=jnp.float32)
    hidden = (jax.nn.silu(gated) * lifted).astype(jnp.bfloat16)
    produced = jnp.dot(hidden, down_weight[0], preferred_element_type=jnp.float32).astype(
        jnp.bfloat16
    )
    return produced.reshape(shape_kept)


def per_device(
    residual_in,
    attention_gain,
    query_weight,
    key_weight,
    value_weight,
    output_weight,
    prompt_keys,
    prompt_values,
    group_index,
    prompt_length,
    own_length,
    expert_gain,
    expert_ids,
    expert_mix,
    gate_weight,
    up_weight,
    down_weight,
):
    tok_rows, width = residual_in.shape
    local_width = query_weight.shape[1]
    heads_here = local_width // HD
    requests = group_index.shape[1]
    longest = prompt_keys.shape[1]
    groups_here = prompt_keys.shape[0]
    normed = rms_scale(residual_in, attention_gain)
    piece = lax.all_gather(normed, "expert", axis=0, tiled=True)
    query_part = jnp.dot(piece, query_weight, preferred_element_type=jnp.float32).astype(
        jnp.bfloat16
    )
    key_part = jnp.dot(piece, key_weight, preferred_element_type=jnp.float32).astype(jnp.bfloat16)
    value_part = jnp.dot(piece, value_weight, preferred_element_type=jnp.float32).astype(
        jnp.bfloat16
    )
    projected = jnp.concatenate([query_part, key_part, value_part], axis=1)
    layout = (requests, SB, heads_here, HD)
    queries = projected[:, :local_width].reshape(layout)
    new_keys = projected[:, local_width : 2 * local_width].reshape(layout)
    new_values = projected[:, 2 * local_width :].reshape(layout)
    scale = HD ** (-0.5)
    positions = jnp.arange(SB, dtype=jnp.int32)
    own_scores = (
        jnp.einsum("rihd,rjhd->rhij", queries, new_keys, preferred_element_type=jnp.float32) * scale
    )
    own_scores = jnp.where(
        positions[None, None, None, :] < own_length[:, None, None, None], own_scores, -jnp.inf
    )
    member = group_index[0]
    prompt_positions = jnp.arange(longest, dtype=jnp.int32)

    def group_step(group, attended):
        first = jnp.sum((member < group).astype(jnp.int32))
        start = jnp.minimum(first, requests - GSIZE)
        window_queries = lax.dynamic_slice_in_dim(queries, start, GSIZE, 0)
        group_keys = lax.dynamic_index_in_dim(prompt_keys, group, 0, keepdims=False).reshape(
            longest, heads_here, HD
        )
        group_values = lax.dynamic_index_in_dim(prompt_values, group, 0, keepdims=False).reshape(
            longest, heads_here, HD
        )
        scores = (
            jnp.einsum(
                "rihd,jhd->rhij", window_queries, group_keys, preferred_element_type=jnp.float32
            )
            * scale
        )
        limit = lax.dynamic_index_in_dim(prompt_length, group, 0, keepdims=False)
        scores = jnp.where(prompt_positions < limit, scores, -jnp.inf)
        window_own = lax.dynamic_slice_in_dim(own_scores, start, GSIZE, 0)
        highest = jnp.maximum(jnp.max(scores, axis=-1), jnp.max(window_own, axis=-1))
        prompt_weights = jnp.exp(scores - highest[..., None]).astype(jnp.bfloat16)
        own_weights = jnp.exp(window_own - highest[..., None]).astype(jnp.bfloat16)
        window_values = lax.dynamic_slice_in_dim(new_values, start, GSIZE, 0)
        summed = jnp.einsum(
            "rhij,jhd->rihd", prompt_weights, group_values, preferred_element_type=jnp.float32
        )
        summed = summed + jnp.einsum(
            "rhij,rjhd->rihd", own_weights, window_values, preferred_element_type=jnp.float32
        )
        totals = jnp.sum(prompt_weights, axis=-1, dtype=jnp.float32) + jnp.sum(
            own_weights, axis=-1, dtype=jnp.float32
        )
        result = (summed / jnp.transpose(totals, (0, 2, 1))[..., None]).astype(jnp.bfloat16)
        inside = lax.dynamic_slice_in_dim(member, start, GSIZE, 0) == group
        current = lax.dynamic_slice_in_dim(attended, start, GSIZE, 0)
        merged = jnp.where(inside[:, None, None, None], result, current)
        return lax.dynamic_update_slice_in_dim(attended, merged, start, 0)

    attended = lax.fori_loop(0, groups_here, group_step, jnp.zeros(layout, jnp.bfloat16))
    flat_attended = attended.reshape(requests * SB, local_width)
    piece = flat_attended
    expert_groups = lax.axis_size("expert")
    projected_out = jnp.dot(piece, output_weight, preferred_element_type=jnp.float32).astype(
        jnp.bfloat16
    )
    partials = lax.all_to_all(
        projected_out.reshape(expert_groups, tok_rows, width), "expert", 0, 0, tiled=True
    )
    attention_update = jnp.sum(partials.astype(jnp.float32), axis=0).astype(jnp.bfloat16)
    expert_input = rms_scale(
        residual_in.astype(jnp.float32) + attention_update.astype(jnp.float32), expert_gain
    )
    data_groups = lax.axis_size("dp")
    devices = data_groups * expert_groups
    hidden_split = FF // gate_weight.shape[2]
    experts = devices // hidden_split
    capacity = max(2, tok_rows * TOP * 3 // (2 * experts))
    chosen = expert_ids.reshape(-1)
    routes_here = chosen.shape[0]
    owners = jnp.arange(routes_here, dtype=jnp.int32) // TOP
    matches = (chosen[:, None] == jnp.arange(experts, dtype=jnp.int32)[None, :]).astype(jnp.int32)
    slots = jnp.sum((jnp.cumsum(matches, axis=0) - matches) * matches, axis=1)
    table = (
        jnp.full((experts * capacity,), tok_rows, jnp.int32)
        .at[chosen * capacity + slots]
        .set(owners)
    )
    lanes = 128
    sub = width // lanes
    tiles = expert_input.reshape(tok_rows, sub, lanes)
    padded = jnp.concatenate([tiles, jnp.zeros((1, sub, lanes), jnp.bfloat16)], axis=0)
    index = jnp.broadcast_to(
        table.reshape(experts, 1, capacity), (experts, hidden_split, capacity)
    ).reshape(-1)
    outgoing = padded[index].reshape(devices, capacity * sub, lanes)
    arrived = lax.all_to_all(outgoing, ("dp", "expert"), 0, 0, tiled=True)
    produced = expert_block(
        arrived.reshape(devices * capacity, width), gate_weight, up_weight, down_weight
    )
    returned = lax.all_to_all(
        produced.reshape(devices, capacity * sub, lanes), ("dp", "expert"), 0, 0, tiled=True
    )
    pieces = returned.reshape(experts, hidden_split, capacity, sub, lanes)[chosen, :, slots]
    blended = jnp.sum(pieces.astype(jnp.float32), axis=1) * expert_mix.reshape(-1)[:, None, None]
    expert_update = (
        jnp.sum(blended.reshape(tok_rows, TOP, sub, lanes), axis=1)
        .reshape(tok_rows, width)
        .astype(jnp.bfloat16)
    )
    return (attention_update, expert_update)


def solution(mesh):
    in_specs = (
        P(("dp", "expert"), None),
        P(),
        P(None, "expert"),
        P(None, "expert"),
        P(None, "expert"),
        P("expert", None),
        P("dp", None, "expert"),
        P("dp", None, "expert"),
        P("dp", None),
        P("dp"),
        P("dp"),
        P(),
        P(("dp", "expert"), None),
        P(("dp", "expert"), None),
        P(("dp", "expert"), None, None),
        P(("dp", "expert"), None, None),
        P(("dp", "expert"), None, None),
    )
    out_specs = (P(("dp", "expert"), None), P(("dp", "expert"), None))
    return jax.shard_map(
        per_device, mesh=mesh, in_specs=in_specs, out_specs=out_specs, check_vma=False
    )
```

profile of v0, /device:TPU:1, one launch (start us, length us, event | category | flops | bytes accessed | tf_op | source)
XLA Modules:
  0.0 408.5 jit_solution(3782199950880802426)
XLA Ops:
  7.2 1.3 fusion.50
  8.5 1.8 fusion.52
  11.1 54.0 %all-gather.2.cloned.1.call-done = bf16[1024,2048]{1,0:T(8,128)(2,1)} async-done(((bf16[64,2048]{1,0:T(8,128)(2,1)}), bf16[1024,2048]{1,0:T(8,128)(2,1)}) %all-gather.2.cloned.1.call-update) | async-done | bytes 4194320 | tf_op jit(solution)/shard_map/all_gather | solution.py:58
  65.1 3.7 convolution_convert_fusion.4
  68.8 1.2 convolution_convert_fusion.3
  70.3 1.2 convolution_convert_fusion.2
  71.7 24.7 %while.14 = (s32[]{:T(128)}, bf16[32,32,1,128]{3,1,0,2:T(8,128)(2,1)S(1)}, s32[32]{0:T(128)S(1)}, bf16[3,2048,128]{2,1,0:T(8,128)(2,1)}, s32[3]{0:T(128)S(1)}, /...) while((s32[]{:T(128)}, ...), condition=%wide.region_7.8_spmd.clone, body=%wide.region_1.7_spmd.clone.sunk | while | flops 555074688 | bytes 15133611 | solution.py:120
  74.2 1.9 bitcast_reduce_fusion.2
  76.2 0.9 convert_reduce_fusion.5
  77.8 2.1 fusion.93
  82.4 1.9 bitcast_reduce_fusion.2
  84.4 0.9 convert_reduce_fusion.5
  86.0 2.1 fusion.93
  90.6 1.9 bitcast_reduce_fusion.2
  92.7 0.9 convert_reduce_fusion.5
  94.3 2.1 fusion.93
  96.3 4.3 %convolution_convert_fusion.1 = bf16[1024,2048]{1,0:T(8,128)(2,1)} fusion(bf16[1024,128]{1,0:T(8,128)(2,1)S(1)} %bitcast.178, bf16[128,2048]{1,0:T(8,128)(2,1)} %param.24), kind=kOutput, calls=%fused_computation.44 | convolution fusion | flops 538968064 | bytes 4980736 | tf_op jit(solution)/shard_map/dot_general | solution.py:124
  100.6 5.2 %all-to-all-start = ((bf16[16,64,2048]{2,1,0:T(8,128)(2,1)}), bf16[16,64,2048]{2,1,0:T(8,128)(2,1)}, u32[]{:S(2)}, u32[]{:S(2)}) async-start(bf16[16,64,2048]{2,1,0:T(8,128)(2,1)} %bitcast.174), calls=%async_computation | async-start | bytes 8388608 | tf_op jit(solution)/shard_map/all_to_all | solution.py:127
  106.2 1.2 reduce-window.6
  107.8 2.4 scatter_custom_fusion
  110.6 54.0 %all-to-all-done = bf16[16,64,2048]{2,1,0:T(8,128)(2,1)} async-done(((bf16[16,64,2048]{2,1,0:T(8,128)(2,1)}), bf16[16,64,2048]{2,1,0:T(8,128)(2,1)}, u32[]{:S(2)}, u32[]{:S(2)}) %all-to-all-start) | async-done | bytes 4194336 | tf_op jit(solution)/shard_map/all_to_all | solution.py:127
  164.6 3.0 reduce_sum.97
  168.0 5.7 %gather_fusion = bf16[1536,16,128]{2,1,0:T(8,128)(2,1)} fusion(bf16[65,16,128]{2,1,0:T(8,128)(2,1)S(1)} %concatenate.6, s32[2048]{0:T(1024)S(1)} %pad_clamp_fusion), kind=kCustom, calls=%fused_computation | custom fusion | bytes 12589056 | tf_op jit(solution)/shard_map/gather | solution.py:156
  173.8 91.0 %all_to_all.15 = bf16[128,192,128]{2,1,0:T(8,128)(2,1)} all-to-all(bf16[128,192,128]{2,1,0:T(8,128)(2,1)} %bitcast.175), channel_id=1, replica_groups=mesh['dp'=8,'expert'=16] {'dp','expert'}, dimensions={0} | all-to-all | bytes 12582912 | tf_op jit(solution)/shard_map/all_to_all | solution.py:157
  264.7 10.3 %reshape.320 = bf16[1536,2048]{1,0:T(8,128)(2,1)} reshape(bf16[128,192,128]{2,1,0:T(8,128)(2,1)} %all_to_all.15) | data formatting | bytes 12582912 | tf_op jit(solution)/shard_map/reshape | solution.py:159
  275.0 8.5 %fusion.44 = f32[1536,512]{1,0:T(8,128)} fusion(bf16[1536,2048]{1,0:T(8,128)(2,1)} %reshape.320, bf16[1,2048,512]{2,1,0:T(8,128)(2,1)} %param.33), kind=kOutput, calls=%fused_computation.49 | convolution fusion | flops 3221225472 | bytes 11534336 | tf_op jit(solution)/shard_map/dot_general | solution.py:23
  283.6 11.7 %convolution_convert_fusion = bf16[1536,2048]{1,0:T(8,128)(2,1)} fusion(bf16[1,512,2048]{2,1,0:T(8,128)(2,1)S(1)} %copy-done, bf16[1536,2048]{1,0:T(8,128)(2,1)} %reshape.320, f32[1536,512]{1,0:T(8,128)} %fusion.44, bf16[1,2048,512]{2,1,0:T(8,128)(2,1)} %param.34), kind=kOutput, calls=%fused_computation.42 | convolution fusion | flops 6450315264 | bytes 19922944 | tf_op jit(solution)/shard_map/dot_general | solution.py:26
  295.3 10.5 %reshape.321 = bf16[128,192,128]{2,1,0:T(8,128)(2,1)} reshape(bf16[1536,2048]{1,0:T(8,128)(2,1)} %convolution_convert_fusion) | data formatting | bytes 12582912 | tf_op jit(solution)/shard_map/reshape | solution.py:162
  305.8 5.6 %all-to-all-start.2 = ((bf16[128,192,128]{2,1,0:T(8,128)(2,1)}), bf16[128,192,128]{2,1,0:T(8,128)(2,1)}, u32[]{:S(2)}, u32[]{:S(2)}) async-start(bf16[128,192,128]{2,1,0:T(8,128)(2,1)} %reshape.321), calls=%async_computation.2 | async-start | bytes 12582912 | tf_op jit(solution)/shard_map/all_to_all | solution.py:161
  311.5 75.4 %all-to-all-done.2 = bf16[128,192,128]{2,1,0:T(8,128)(2,1)} async-done(((bf16[128,192,128]{2,1,0:T(8,128)(2,1)}), bf16[128,192,128]{2,1,0:T(8,128)(2,1)}, u32[]{:S(2)}, u32[]{:S(2)}) %all-to-all-start.2) | async-done | bytes 6291488 | tf_op jit(solution)/shard_map/all_to_all | solution.py:161
  386.9 8.9 %gather_fusion.1 = bf16[512,2,16,128]{3,2,1,0:T(8,128)(2,1)} fusion(bf16[64,2,12,16,128]{4,3,2,1,0:T(8,128)(2,1)} %bitcast.15, s32[512]{0:T(512)S(1)} %bitcast.173), kind=kCustom, calls=%fused_computation.1 | custom fusion | bytes 8392704 | tf_op jit(solution)/shard_map/gather | solution.py:164
  395.8 4.1 %convert_reduce_fusion.2 = f32[512,16,128]{2,1,0:T(8,128)S(1)} fusion(bf16[512,2,16,128]{3,2,1,0:T(8,128)(2,1)} %gather_fusion.1), kind=kLoop, calls=%fused_computation.41 | loop fusion | flops 3145728 | bytes 8388608 | tf_op jit(solution)/shard_map/reduce_sum | solution.py:165
  (79 shorter events, 12.2 us)
Async XLA Ops:
  7.2 276.4 %copy-start = (bf16[1,512,2048]{2,1,0:T(8,128)(2,1)S(1)}, bf16[1,512,2048]{2,1,0:T(8,128)(2,1)}, u32[]{:S(2)}) copy-start(bf16[1,512,2048]{2,1,0:T(8,128)(2,1)} %param.35) | copy-start | bytes 6291460
  7.2 61.6 %copy-start.8 = (bf16[2048,128]{1,0:T(8,128)(2,1)S(1)}, bf16[2048,128]{1,0:T(8,128)(2,1)}, u32[]{:S(2)}) copy-start(bf16[2048,128]{1,0:T(8,128)(2,1)} %param.22) | copy-start | bytes 1572868
  7.2 57.9 %all-gather.2.cloned.1.call-start = ((), (), s32[]{:S(2)}) async-start(), calls=%async_computation.3 | async-start | bytes 4456448 | tf_op jit(solution)/shard_map/all_gather | solution.py:58
  65.1 3.7 copy-start.7
  68.8 1.6 copy-start.9
  70.0 1.6 copy-start.3
  70.1 1.6 copy-start.10
  100.6 5.2 %copy-start.5 = (s32[64,8]{0,1:T(8,128)S(1)}, s32[64,8]{0,1:T(8,128)}, u32[]{:S(2)}) copy-start(s32[64,8]{0,1:T(8,128)} %param.31) | copy-start | bytes 6148
  100.6 64.0 %all-to-all-start = ((bf16[16,64,2048]{2,1,0:T(8,128)(2,1)}), bf16[16,64,2048]{2,1,0:T(8,128)(2,1)}, u32[]{:S(2)}, u32[]{:S(2)}) async-start(bf16[16,64,2048]{2,1,0:T(8,128)(2,1)} %bitcast.174), calls=%async_computation | async-start | bytes 8388608 | tf_op jit(solution)/shard_map/all_to_all | solution.py:127
  105.8 61.8 %copy-start.1 = (bf16[64,2048]{1,0:T(8,128)(2,1)S(1)}, bf16[64,2048]{1,0:T(8,128)(2,1)}, u32[]{:S(2)}) copy-start(bf16[64,2048]{1,0:T(8,128)(2,1)} %param.19) | copy-start | bytes 786436
  105.8 62.0 %copy-start.4 = (f32[2048]{0:T(1024)S(1)}, f32[2048]{0:T(1024)}, u32[]{:S(2)}) copy-start(f32[2048]{0:T(1024)} %param.30) | copy-start | bytes 24580
  167.6 6.1 %copy-start.2 = (bf16[64,2048]{1,0:T(8,128)(2,1)}, bf16[64,2048]{1,0:T(8,128)(2,1)S(1)}, u32[]{:S(2)}) copy-start(bf16[64,2048]{1,0:T(8,128)(2,1)S(1)} %reduce_sum.97) | copy-start | bytes 786436
  305.8 5.6 %copy-start.6 = (f32[64,8]{0,1:T(8,128)S(1)}, f32[64,8]{0,1:T(8,128)}, u32[]{:S(2)}) copy-start(f32[64,8]{0,1:T(8,128)} %param.32) | copy-start | bytes 6148
  305.8 81.2 %all-to-all-start.2 = ((bf16[128,192,128]{2,1,0:T(8,128)(2,1)}), bf16[128,192,128]{2,1,0:T(8,128)(2,1)}, u32[]{:S(2)}, u32[]{:S(2)}) async-start(bf16[128,192,128]{2,1,0:T(8,128)(2,1)} %reshape.321), calls=%async_computation.2 | async-start | bytes 12582912 | tf_op jit(solution)/shard_map/all_to_all | solution.py:161
Sparse Core Ops, SparseCore 0:
  10.7 54.2 all-gather.1
where the time goes:
time: 410 us; the launch traced here: 408 us
  waiting for transfers between devices  183 us (45%)
  blocking collectives  91 us (22%)
  matrix products  43.5 us (11%)
  local copies, waits for them, and re-layouts  41.5 us (10%)
  other arithmetic  21.8 us (5%)
  between operations  14.3 us (3%)
  starting transfers between devices  10.8 us (3%)
    all_to_all x1, blocking collectives, per_device(): arrived = lax.all_to_all(outgoing, ('dp', 'expert'), 0, 0, tiled=True)  91 us
    all_to_all x1, waiting for transfers between devices, per_device(): lax.all_to_all(produced.reshape(devices, capacity * sub, lanes), ('dp', '...  75.4 us
    all_to_all x1, waiting for transfers between devices, per_device(): lax.all_to_all(projected_out.reshape(expert_groups, tok_rows, width), 'ex...  54 us
    all_gather x1, waiting for transfers between devices, per_device(): piece = lax.all_gather(normed, 'expert', axis=0, tiled=True)  54 us
    dot_general x1, matrix products, expert_block(): jnp.dot(hidden, down_weight[0], preferred_element_type=jnp.float32)  11.7 us
    reshape x1, local copies, waits for them, and re-layouts, per_device(): produced.reshape(devices, capacity * sub, lanes)  10.5 us
    reshape x1, local copies, waits for them, and re-layouts, per_device(): arrived.reshape(devices * capacity, width)  10.3 us
    gather x1, local copies, waits for them, and re-layouts, per_device(): returned.reshape(experts, hidden_split, capacity, sub, lanes)  8.94 us
  transfers between devices with their start and end apart: 3, of which 3 were waited for; matrix products, arithmetic and copies ran while one was open for 1% of the time, Pallas kernels for 0%

commit v1 on v0

--- a/solution.py
+++ b/solution.py
@@ -1,3 +1,4 @@
+import functools
 import jax
 import jax.numpy as jnp
 from jax import lax
@@ -9,6 +10,17 @@
 GSIZE = 16
 SB = 32
 epsilon = 1e-06
+
+
+def samples_all_clear(matrix, along_dim):
+    a_next = jnp.concatenate(
+        lax.all_to_all(jnp.stack([matrix] * lax.axis_size("expert")), "expert", 0, 0),
+        axis=along_dim,
+    )
+    return a_next
+
+
+turn_row = functools.partial(samples_all_clear, along_dim=0)
 
 
 def rms_scale(values, gain):
@@ -55,7 +67,7 @@
     longest = prompt_keys.shape[1]
     groups_here = prompt_keys.shape[0]
     normed = rms_scale(residual_in, attention_gain)
-    piece = lax.all_gather(normed, "expert", axis=0, tiled=True)
+    piece = turn_row(normed)
     query_part = jnp.dot(piece, query_weight, preferred_element_type=jnp.float32).astype(
         jnp.bfloat16
     )

time: 410 us -> 411 us (level)
  starting transfers between devices: 10.8 us -> 25 us
  between operations: 14.3 us -> 0.94 us
  matrix products: 43.5 us -> 47.8 us
    all_to_all x0 -> x1, waiting for transfers between devices: none -> 60.2 us  [samples_all_clear(): lax.all_to_all(jnp.stack([matrix] * lax.axis_size('expert')), 'expert', 0...]
    all_gather x1 -> x0, waiting for transfers between devices: 54 us -> none  [per_device(): piece = lax.all_gather(normed, 'expert', axis=0, tiled=True)]
    all_to_all x0 -> x1, starting transfers between devices: none -> 7.76 us  [samples_all_clear(): lax.all_to_all(jnp.stack([matrix] * lax.axis_size('expert')), 'expert', 0...]
    all_to_all x1, waiting for transfers between devices: 54 us -> 46.6 us  [per_device(): lax.all_to_all(projected_out.reshape(expert_groups, tok_rows, width), 'ex...]
    all_to_all x1, starting transfers between devices: 5.17 us -> 11.6 us  [per_device(): lax.all_to_all(projected_out.reshape(expert_groups, tok_rows, width), 'ex...]
where the time goes in v1:
time: 411 us; the launch traced here: 410 us
  waiting for transfers between devices  182 us (44%)
  blocking collectives  87.2 us (21%)
  matrix products  47.8 us (12%)
  local copies, waits for them, and re-layouts  44 us (11%)
  starting transfers between devices  25 us (6%)
  other arithmetic  20.4 us (5%)
    all_to_all x1, blocking collectives, per_device(): arrived = lax.all_to_all(outgoing, ('dp', 'expert'), 0, 0, tiled=True)  87.2 us
    all_to_all x1, waiting for transfers between devices, per_device(): lax.all_to_all(produced.reshape(devices, capacity * sub, lanes), ('dp', '...  75.4 us
    all_to_all x1, waiting for transfers between devices, samples_all_clear(): lax.all_to_all(jnp.stack([matrix] * lax.axis_size('expert')), 'expert', 0...  60.2 us
    all_to_all x1, waiting for transfers between devices, per_device(): lax.all_to_all(projected_out.reshape(expert_groups, tok_rows, width), 'ex...  46.6 us
    dot_general x1, matrix products, expert_block(): jnp.dot(hidden, down_weight[0], preferred_element_type=jnp.float32)  11.7 us
    all_to_all x1, starting transfers between devices, per_device(): lax.all_to_all(projected_out.reshape(expert_groups, tok_rows, width), 'ex...  11.6 us
    reshape x1, local copies, waits for them, and re-layouts, per_device(): produced.reshape(devices, capacity * sub, lanes)  10.5 us
    reshape x1, local copies, waits for them, and re-layouts, per_device(): arrived.reshape(devices * capacity, width)  10.3 us
  transfers between devices with their start and end apart: 3, of which 3 were waited for; matrix products, arithmetic and copies ran while one was open for 1% of the time, Pallas kernels for 0%

profile of v1, /device:TPU:1, one launch (start us, length us, event | category | flops | bytes accessed | tf_op | source)
XLA Modules:
  0.0 409.8 jit_solution(16017133245089518491)
XLA Ops:
  0.6 1.3 fusion.50
  1.9 1.1 fusion.52
  3.0 2.5 stack.2
  5.5 7.8 %all-to-all-start = ((bf16[16,64,2048]{2,1,0:T(8,128)(2,1)}), bf16[16,64,2048]{2,1,0:T(8,128)(2,1)}, u32[]{:S(2)}, u32[]{:S(2)}) async-start(bf16[16,64,2048]{2,1,0:T(8,128)(2,1)} %stack.2), calls=%async_computation | async-start | bytes 8388608 | tf_op jit(solution)/shard_map/all_to_all | solution.py:17
  13.4 60.2 %all-to-all-done = bf16[16,64,2048]{2,1,0:T(8,128)(2,1)} async-done(((bf16[16,64,2048]{2,1,0:T(8,128)(2,1)}), bf16[16,64,2048]{2,1,0:T(8,128)(2,1)}, u32[]{:S(2)}, u32[]{:S(2)}) %all-to-all-start) | async-done | bytes 4194336 | tf_op jit(solution)/shard_map/all_to_all | solution.py:17
  73.6 3.4 convolution_convert_fusion.4
  77.0 3.6 convolution_convert_fusion.3
  80.7 3.4 convolution_convert_fusion.2
  84.5 24.7 %while.14 = (s32[]{:T(128)}, bf16[32,32,1,128]{3,1,0,2:T(8,128)(2,1)S(1)}, s32[32]{0:T(128)S(1)}, bf16[3,2048,128]{2,1,0:T(8,128)(2,1)}, s32[3]{0:T(128)S(1)}, /...) while((s32[]{:T(128)}, ...), condition=%wide.region_7.8_spmd.clone, body=%wide.region_1.7_spmd.clone.sunk | while | flops 555074688 | bytes 15133611 | solution.py:132
  87.0 1.9 bitcast_reduce_fusion.2
  90.6 2.1 fusion.93
  95.2 1.9 bitcast_reduce_fusion.2
  97.3 0.9 convert_reduce_fusion.5
  98.8 2.1 fusion.93
  103.5 1.9 bitcast_reduce_fusion.2
  107.1 2.1 fusion.93
  109.1 4.3 %convolution_convert_fusion.1 = bf16[1024,2048]{1,0:T(8,128)(2,1)} fusion(bf16[1024,128]{1,0:T(8,128)(2,1)S(1)} %bitcast.179, bf16[128,2048]{1,0:T(8,128)(2,1)} %param.24), kind=kOutput, calls=%fused_computation.44 | convolution fusion | flops 538968064 | bytes 4980736 | tf_op jit(solution)/shard_map/dot_general | solution.py:136
  113.4 11.6 %all-to-all-start.1 = ((bf16[16,64,2048]{2,1,0:T(8,128)(2,1)}), bf16[16,64,2048]{2,1,0:T(8,128)(2,1)}, u32[]{:S(2)}, u32[]{:S(2)}) async-start(bf16[16,64,2048]{2,1,0:T(8,128)(2,1)} %bitcast.175), calls=%async_computation.1 | async-start | bytes 8388608 | tf_op jit(solution)/shard_map/all_to_all | solution.py:139
  125.4 1.2 reduce-window.6
  127.0 2.4 scatter_custom_fusion
  129.8 46.6 %all-to-all-done.1 = bf16[16,64,2048]{2,1,0:T(8,128)(2,1)} async-done(((bf16[16,64,2048]{2,1,0:T(8,128)(2,1)}), bf16[16,64,2048]{2,1,0:T(8,128)(2,1)}, u32[]{:S(2)}, u32[]{:S(2)}) %all-to-all-start.1) | async-done | bytes 4194336 | tf_op jit(solution)/shard_map/all_to_all | solution.py:139
  176.4 3.0 reduce_sum.97
  179.8 5.7 %gather_fusion = bf16[1536,16,128]{2,1,0:T(8,128)(2,1)} fusion(bf16[65,16,128]{2,1,0:T(8,128)(2,1)S(1)} %concatenate.6, s32[2048]{0:T(1024)S(1)} %pad_clamp_fusion), kind=kCustom, calls=%fused_computation | custom fusion | bytes 12589056 | tf_op jit(solution)/shard_map/gather | solution.py:168
  185.6 87.2 %all_to_all.20 = bf16[128,192,128]{2,1,0:T(8,128)(2,1)} all-to-all(bf16[128,192,128]{2,1,0:T(8,128)(2,1)} %bitcast.176), channel_id=1, replica_groups=mesh['dp'=8,'expert'=16] {'dp','expert'}, dimensions={0} | all-to-all | bytes 12582912 | tf_op jit(solution)/shard_map/all_to_all | solution.py:169
  272.8 10.3 %reshape.326 = bf16[1536,2048]{1,0:T(8,128)(2,1)} reshape(bf16[128,192,128]{2,1,0:T(8,128)(2,1)} %all_to_all.20) | data formatting | bytes 12582912 | tf_op jit(solution)/shard_map/reshape | solution.py:171
  283.1 8.5 %fusion.44 = f32[1536,512]{1,0:T(8,128)} fusion(bf16[1536,2048]{1,0:T(8,128)(2,1)} %reshape.326, bf16[1,2048,512]{2,1,0:T(8,128)(2,1)} %param.33), kind=kOutput, calls=%fused_computation.49 | convolution fusion | flops 3221225472 | bytes 11534336 | tf_op jit(solution)/shard_map/dot_general | solution.py:35
  291.6 11.7 %convolution_convert_fusion = bf16[1536,2048]{1,0:T(8,128)(2,1)} fusion(bf16[1,512,2048]{2,1,0:T(8,128)(2,1)S(1)} %copy-done, bf16[1536,2048]{1,0:T(8,128)(2,1)} %reshape.326, f32[1536,512]{1,0:T(8,128)} %fusion.44, bf16[1,2048,512]{2,1,0:T(8,128)(2,1)} %param.34), kind=kOutput, calls=%fused_computation.42 | convolution fusion | flops 6450315264 | bytes 19922944 | tf_op jit(solution)/shard_map/dot_general | solution.py:38
  303.4 10.5 %reshape.327 = bf16[128,192,128]{2,1,0:T(8,128)(2,1)} reshape(bf16[1536,2048]{1,0:T(8,128)(2,1)} %convolution_convert_fusion) | data formatting | bytes 12582912 | tf_op jit(solution)/shard_map/reshape | solution.py:174
  313.8 5.7 %all-to-all-start.3 = ((bf16[128,192,128]{2,1,0:T(8,128)(2,1)}), bf16[128,192,128]{2,1,0:T(8,128)(2,1)}, u32[]{:S(2)}, u32[]{:S(2)}) async-start(bf16[128,192,128]{2,1,0:T(8,128)(2,1)} %reshape.327), calls=%async_computation.3 | async-start | bytes 12582912 | tf_op jit(solution)/shard_map/all_to_all | solution.py:173
  319.6 75.4 %all-to-all-done.3 = bf16[128,192,128]{2,1,0:T(8,128)(2,1)} async-done(((bf16[128,192,128]{2,1,0:T(8,128)(2,1)}), bf16[128,192,128]{2,1,0:T(8,128)(2,1)}, u32[]{:S(2)}, u32[]{:S(2)}) %all-to-all-start.3) | async-done | bytes 6291488 | tf_op jit(solution)/shard_map/all_to_all | solution.py:173
  395.0 8.9 %gather_fusion.1 = bf16[512,2,16,128]{3,2,1,0:T(8,128)(2,1)} fusion(bf16[64,2,12,16,128]{4,3,2,1,0:T(8,128)(2,1)} %bitcast.16, s32[512]{0:T(512)S(1)} %bitcast.174), kind=kCustom, calls=%fused_computation.1 | custom fusion | bytes 8392704 | tf_op jit(solution)/shard_map/gather | solution.py:176
  404.0 4.1 %convert_reduce_fusion.2 = f32[512,16,128]{2,1,0:T(8,128)S(1)} fusion(bf16[512,2,16,128]{3,2,1,0:T(8,128)(2,1)} %gather_fusion.1), kind=kLoop, calls=%fused_computation.41 | loop fusion | flops 3145728 | bytes 8388608 | tf_op jit(solution)/shard_map/reduce_sum | solution.py:177
  (79 shorter events, 13.4 us)
Async XLA Ops:
  0.6 291.0 %copy-start = (bf16[1,512,2048]{2,1,0:T(8,128)(2,1)S(1)}, bf16[1,512,2048]{2,1,0:T(8,128)(2,1)}, u32[]{:S(2)}) copy-start(bf16[1,512,2048]{2,1,0:T(8,128)(2,1)} %param.35) | copy-start | bytes 6291460
  5.5 7.8 %copy-start.7 = (s32[32]{0:T(128)S(1)}, s32[32]{0:T(128)}, u32[]{:S(2)}) copy-start(s32[32]{0:T(128)} %param.29) | copy-start | bytes 388
  5.5 68.1 %copy-start.8 = (bf16[2048,128]{1,0:T(8,128)(2,1)S(1)}, bf16[2048,128]{1,0:T(8,128)(2,1)}, u32[]{:S(2)}) copy-start(bf16[2048,128]{1,0:T(8,128)(2,1)} %param.21) | copy-start | bytes 1572868
  5.5 68.1 %all-to-all-start = ((bf16[16,64,2048]{2,1,0:T(8,128)(2,1)}), bf16[16,64,2048]{2,1,0:T(8,128)(2,1)}, u32[]{:S(2)}, u32[]{:S(2)}) async-start(bf16[16,64,2048]{2,1,0:T(8,128)(2,1)} %stack.2), calls=%async_computation | async-start | bytes 8388608 | tf_op jit(solution)/shard_map/all_to_all | solution.py:17
  77.0 3.6 copy-start.9
  80.7 3.8 copy-start.3
  80.7 3.8 copy-start.10
  113.4 11.6 %copy-start.5 = (s32[64,8]{0,1:T(8,128)S(1)}, s32[64,8]{0,1:T(8,128)}, u32[]{:S(2)}) copy-start(s32[64,8]{0,1:T(8,128)} %param.31) | copy-start | bytes 6148
  113.4 63.0 %all-to-all-start.1 = ((bf16[16,64,2048]{2,1,0:T(8,128)(2,1)}), bf16[16,64,2048]{2,1,0:T(8,128)(2,1)}, u32[]{:S(2)}, u32[]{:S(2)}) async-start(bf16[16,64,2048]{2,1,0:T(8,128)(2,1)} %bitcast.175), calls=%async_computation.1 | async-start | bytes 8388608 | tf_op jit(solution)/shard_map/all_to_all | solution.py:139
  125.0 54.4 %copy-start.1 = (bf16[64,2048]{1,0:T(8,128)(2,1)S(1)}, bf16[64,2048]{1,0:T(8,128)(2,1)}, u32[]{:S(2)}) copy-start(bf16[64,2048]{1,0:T(8,128)(2,1)} %param.19) | copy-start | bytes 786436
  125.0 54.6 %copy-start.4 = (f32[2048]{0:T(1024)S(1)}, f32[2048]{0:T(1024)}, u32[]{:S(2)}) copy-start(f32[2048]{0:T(1024)} %param.30) | copy-start | bytes 24580
  179.4 6.1 %copy-start.2 = (bf16[64,2048]{1,0:T(8,128)(2,1)}, bf16[64,2048]{1,0:T(8,128)(2,1)S(1)}, u32[]{:S(2)}) copy-start(bf16[64,2048]{1,0:T(8,128)(2,1)S(1)} %reduce_sum.97) | copy-start | bytes 786436
  313.8 5.7 %copy-start.6 = (f32[64,8]{0,1:T(8,128)S(1)}, f32[64,8]{0,1:T(8,128)}, u32[]{:S(2)}) copy-start(f32[64,8]{0,1:T(8,128)} %param.32) | copy-start | bytes 6148
  313.8 81.2 %all-to-all-start.3 = ((bf16[128,192,128]{2,1,0:T(8,128)(2,1)}), bf16[128,192,128]{2,1,0:T(8,128)(2,1)}, u32[]{:S(2)}, u32[]{:S(2)}) async-start(bf16[128,192,128]{2,1,0:T(8,128)(2,1)} %reshape.327), calls=%async_computation.3 | async-start | bytes 12582912 | tf_op jit(solution)/shard_map/all_to_all | solution.py:173
